TPU v7x, 32 devices: a whole 2x2x4 slice. The times are simulated.
32 devices in a mesh: mem: 4 (over z), tile: 8 (over y, x, core).
Axes of the slice: x: 2, y: 2, z: 4, core: 2. Of those that a mesh axis runs over, the one named last changes fastest.
Arguments:
- source_blocks: bfloat16 [1024, 8, 2, 256], P('tile', 'mem'), may hold values from -6 to 6
- send_blocks: int32 [8, 8, 24], P('tile'), may hold values from 0 to 127
- recv_slot: int32 [8, 8, 24], P('tile'), may hold values from 0 to 95
- recv_weight: float32 [8, 8, 24], P('tile'), may hold values from 0.25 to 2
- recv_count: int32 [8, 8], P('tile'), may hold values from 0 to 24, as said below
- regional: bfloat16 [8, 2, 512, 384], P('mem', None, 'tile'), may hold values from -6 to 6
- x_operator: bfloat16 [512, 512], P(('mem', 'tile'))
- y_operator: bfloat16 [384, 384], P(('mem', 'tile'))
Outputs:
- blended: bfloat16 [8, 2, 512, 384], P('mem', None, 'tile')
Inputs may be any that keep to these rules, and one draw needn't show every extreme that they name: `recv_count`: live entries of one pair of tiles number at most 24; some pairs in every draw have 24.
All inputs are finite; a program needn't handle non-finite values.
Results may differ from a plain program's by a relative error of at most 0.0055.
Values may be sent and summed in bfloat16 or wider, within the bound.
No kernel may reach another device: no remote copies, remote signals or barrier semaphores. Data moves between devices by JAX's collectives and lax.ppermute only.
A program may use at most 128 MiB of HBM per device.

v0:
```python
import math
import jax
import jax.numpy as jnp
from jax import lax
from jax.sharding import PartitionSpec as P


def body(
    source_blocks, send_blocks, recv_slot, recv_weight, recv_count, regional, x_operator, y_operator
):
    tile_count = lax.axis_size("tile")
    member_count, level_count, columns, y_cells = regional.shape
    capacity = send_blocks.shape[2]
    block_cells = source_blocks.shape[3]
    block_side = math.isqrt(block_cells)
    picked = send_blocks[0].reshape(-1)
    packed = jnp.take(source_blocks, picked, axis=0).reshape(
        tile_count, capacity, member_count, level_count, block_cells
    )
    arrived = lax.all_to_all(packed, "tile", split_axis=0, concat_axis=0, tiled=True)
    slot_count = columns // block_side * (y_cells // block_side)
    live_mask = lax.broadcasted_iota(jnp.int32, (tile_count, capacity), 1) < recv_count[0][:, None]
    weights = jnp.where(live_mask, recv_weight[0], 0.0).reshape(-1)
    slot_match = recv_slot[0].reshape(-1)[None, :] == lax.broadcasted_iota(
        jnp.int32, (slot_count, tile_count * capacity), 0
    )
    remap_weights = jnp.where(slot_match, weights[None, :], 0.0).astype(jnp.bfloat16)
    remapped = jnp.dot(
        remap_weights,
        arrived.reshape(tile_count * capacity, -1),
        preferred_element_type=jnp.float32,
    )
    remapped = remapped.reshape(
        columns // block_side,
        y_cells // block_side,
        member_count,
        level_count,
        block_side,
        block_side,
    )
    remapped = remapped.transpose(2, 3, 0, 4, 1, 5).reshape(
        member_count, level_count, columns, y_cells
    )
    difference = (remapped - regional.astype(jnp.float32)).astype(jnp.bfloat16)
    x_lines = lax.all_to_all(difference, "tile", split_axis=3, concat_axis=2, tiled=True)
    after_first = jnp.einsum(
        "ax,mlxy->mlay",
        lax.all_gather(x_operator, ("mem", "tile"), axis=0, tiled=True),
        x_lines,
        preferred_element_type=jnp.float32,
    ).astype(jnp.bfloat16)
    tile_back = lax.all_to_all(after_first, "tile", split_axis=2, concat_axis=3, tiled=True)
    after_second = jnp.einsum(
        "by,mlxy->mlxb",
        lax.all_gather(y_operator, ("mem", "tile"), axis=0, tiled=True),
        tile_back,
        preferred_element_type=jnp.float32,
    )
    return (regional.astype(jnp.float32) + after_second).astype(jnp.bfloat16)


def solution(mesh):
    placed = (
        P("tile", "mem", None, None),
        P("tile", None, None),
        P("tile", None, None),
        P("tile", None, None),
        P("tile", None),
        P("mem", None, "tile", None),
        P(("mem", "tile"), None),
        P(("mem", "tile"), None),
    )
    return jax.shard_map(
        body, mesh=mesh, in_specs=placed, out_specs=P("mem", None, "tile", None), check_vma=False
    )
```

profile of v0, /device:TPU:0, one launch (start us, length us, event | category | flops | bytes accessed | tf_op | source)
XLA Modules:
  0.0 121.7 jit_solution(16398745087015653898)
XLA Ops:
  0.0 0.0 copy-start
  0.0 0.0 copy-start.6
  0.0 0.0 copy-start.5
  0.0 0.0 copy-start.4
  0.0 0.8 reshape_squeeze.6
  0.8 0.7 compare_and_fusion
  1.5 0.0 copy-done
  1.5 1.4 %gather_fusion = bf16[192,2,2,256]{3,2,1,0:T(2,128)(2,1)S(1)} fusion(bf16[128,2,2,256]{3,2,1,0:T(2,128)(2,1)S(1)} %copy-done, s32[1024]{0:T(1024)S(1)} %pad_clamp_fusion), kind=kCustom, calls=%fused_computation | custom fusion | bytes 787200 | tf_op jit(solution)/shard_map/jit(_take)/gather | solution.py:17
  3.0 1.2 broadcast_select_fusion
  4.2 5.2 %all-to-all-start = ((bf16[8,24,2,2,256]{4,3,2,1,0:T(2,128)(2,1)}), bf16[8,24,2,2,256]{4,3,2,1,0:T(2,128)(2,1)S(1)}, u32[]{:S(2)}, u32[]{:S(2)}) async-start(bf16[8,24,2,2,256]{4,3,2,1,0:T(2,128)(2,1)} %broadcast_select_fusion), calls=%async_computation | async-start | bytes 786432 | tf_op jit(solution)/shard_map/all_to_all | solution.py:20
  9.4 0.0 copy-done.6
  9.4 0.1 iota_compare_fusion
  9.4 0.1 lt.42
  9.5 0.0 copy-done.5
  9.5 0.1 squeeze.3
  9.6 0.0 copy-done.4
  9.6 0.1 eq.15
  9.7 8.0 %all-to-all-done = bf16[8,24,2,2,256]{4,3,2,1,0:T(2,128)(2,1)S(1)} async-done(((bf16[8,24,2,2,256]{4,3,2,1,0:T(2,128)(2,1)}), bf16[8,24,2,2,256]{4,3,2,1,0:T(2,128)(2,1)S(1)}, u32[]{:S(2)}, u32[]{:S(2)}) %all-to-all-start) | async-done | bytes 393248 | tf_op jit(solution)/shard_map/all_to_all | solution.py:20
  17.7 0.3 reshape.92
  18.0 0.2 copy.16
  18.2 1.9 %convolution_bitcast_fusion = f32[2,2,4,16,24,16]{4,5,3,1,0,2:T(8,128)} fusion(bf16[2,2,16,16,192,1]{4,3,2,1,0,5:T(8,128)(2,1)S(1)} %bitcast.53, bf16[192]{0:T(256)(128)(2,1)S(1)} %broadcast_select_fusion.1, s32[4,24]{1,0:T(4,128)S(1)} %multiply_add_fusion, s32[192]{0:T(256)S(1)} %eq.15), kind=kOutput, calls=%fused_computation.1 | convolution fusion | flops 37785600 | bytes 787968 | tf_op jit(solution)/shard_map/dot_general | solution.py:28
  20.0 2.2 %copy.17 = f32[2,2,4,16,24,16]{5,4,3,2,1,0:T(8,128)S(1)} copy(f32[2,2,4,16,24,16]{4,5,3,1,0,2:T(8,128)} %convolution_bitcast_fusion) | data formatting | bytes 786432 | tf_op jit(solution)/shard_map/transpose | solution.py:41
  22.3 0.0 copy-start.2
  22.3 1.6 %reshape.93 = f32[2,2,64,384]{3,2,1,0:T(8,128)} reshape(f32[2,2,4,16,24,16]{5,4,3,2,1,0:T(8,128)S(1)} %copy.17) | data formatting | bytes 786432 | tf_op jit(solution)/shard_map/reshape | solution.py:41
  23.9 1.1 fusion.3
  25.0 0.6 copy.18
  25.6 1.0 reshape.109
  26.6 3.4 %all-to-all-start.1 = ((bf16[8,2,6144]{2,1,0:T(2,128)(2,1)}), bf16[8,2,6144]{2,1,0:T(2,128)(2,1)S(1)}, u32[]{:S(2)}, u32[]{:S(2)}) async-start(bf16[8,2,6144]{2,1,0:T(2,128)(2,1)} %reshape.109), calls=%async_computation.1 | async-start | bytes 393216 | tf_op jit(solution)/shard_map/all_to_all | solution.py:45
  30.0 0.0 copy-done.2
  30.0 43.6 %all_gather.6 = bf16[512,512]{1,0:T(8,128)(2,1)S(1)} all-gather(bf16[16,512]{1,0:T(8,128)(2,1)S(1)} %copy-done.2), channel_id=1, replica_groups=mesh['mem'=4,'tile'=8] {'mem','tile'}, dimensions={0}, use_global_device_ids=true | all-gather | bytes 540672 | tf_op jit(solution)/shard_map/all_gather | solution.py:48
  73.6 0.0 all-to-all-done.1
  73.6 0.3 reshape.110
  73.9 0.0 copy-start.3
  73.9 0.3 copy.31
  74.2 0.3 all_to_all.33
  74.4 0.3 fusion.1
  74.8 0.4 copy.21
  75.2 1.4 %reshape.111 = bf16[8,2,6144]{2,1,0:T(2,128)(2,1)} reshape(bf16[512,2,2,48]{3,2,1,0:T(2,128)(2,1)S(1)} %bitcast.54) | data formatting | bytes 393216
  76.6 0.0 copy-start.1
  76.6 3.5 %all-to-all-start.2 = ((bf16[8,2,6144]{2,1,0:T(2,128)(2,1)}), bf16[8,2,6144]{2,1,0:T(2,128)(2,1)S(1)}, u32[]{:S(2)}, u32[]{:S(2)}) async-start(bf16[8,2,6144]{2,1,0:T(2,128)(2,1)} %reshape.111), calls=%async_computation.2 | async-start | bytes 393216 | tf_op jit(solution)/shard_map/all_to_all | solution.py:52
  80.1 0.0 copy-done.3
  80.1 39.3 %all-gather = bf16[32,12,384]{2,1,0:T(8,128)(2,1)S(1)} all-gather(bf16[1,12,384]{2,1,0:T(8,128)(2,1)S(1)} %bitcast.62), channel_id=1, replica_groups=mesh['mem'=4,'tile'=8] {'mem','tile'}, dimensions={0}, use_global_device_ids=true | all-gather | bytes 304128 | tf_op jit(solution)/shard_map/all_gather | solution.py:55
  119.4 0.1 reshape.107
  119.5 0.0 all-to-all-done.2
  119.5 0.5 reshape.112
  120.0 0.3 copy.30
  120.4 0.4 all_to_all.37
  120.8 0.0 copy-done.1
  120.8 1.0 fusion
  (4 shorter events, 0.0 us)
Async XLA Ops:
  0.0 1.5 %copy-start = (bf16[128,2,2,256]{3,2,1,0:T(2,128)(2,1)S(1)}, bf16[128,2,2,256]{3,2,1,0:T(2,128)(2,1)}, u32[]{:S(2)}) copy-start(bf16[128,2,2,256]{3,2,1,0:T(2,128)(2,1)} %param.8) | copy-start | bytes 786436
  0.0 9.4 %copy-start.6 = (s32[1,8]{1,0:T(1,128)S(1)}, s32[1,8]{1,0:T(1,128)}, u32[]{:S(2)}) copy-start(s32[1,8]{1,0:T(1,128)} %param.12) | copy-start | bytes 100
  0.0 9.5 %copy-start.5 = (f32[1,8,24]{2,1,0:T(8,128)S(1)}, f32[1,8,24]{2,1,0:T(8,128)}, u32[]{:S(2)}) copy-start(f32[1,8,24]{2,1,0:T(8,128)} %param.11) | copy-start | bytes 2308
  0.0 9.6 %copy-start.4 = (s32[1,8,24]{2,1,0:T(8,128)S(1)}, s32[1,8,24]{2,1,0:T(8,128)}, u32[]{:S(2)}) copy-start(s32[1,8,24]{2,1,0:T(8,128)} %param.10) | copy-start | bytes 2308
  4.2 13.5 %all-to-all-start = ((bf16[8,24,2,2,256]{4,3,2,1,0:T(2,128)(2,1)}), bf16[8,24,2,2,256]{4,3,2,1,0:T(2,128)(2,1)S(1)}, u32[]{:S(2)}, u32[]{:S(2)}) async-start(bf16[8,24,2,2,256]{4,3,2,1,0:T(2,128)(2,1)} %broadcast_select_fusion), calls=%async_computation | async-start | bytes 786432 | tf_op jit(solution)/shard_map/all_to_all | solution.py:20
  22.3 7.7 %copy-start.2 = (bf16[16,512]{1,0:T(8,128)(2,1)S(1)}, bf16[16,512]{1,0:T(8,128)(2,1)}, u32[]{:S(2)}) copy-start(bf16[16,512]{1,0:T(8,128)(2,1)} %param.14) | copy-start | bytes 49156
  26.6 47.0 %all-to-all-start.1 = ((bf16[8,2,6144]{2,1,0:T(2,128)(2,1)}), bf16[8,2,6144]{2,1,0:T(2,128)(2,1)S(1)}, u32[]{:S(2)}, u32[]{:S(2)}) async-start(bf16[8,2,6144]{2,1,0:T(2,128)(2,1)} %reshape.109), calls=%async_computation.1 | async-start | bytes 393216 | tf_op jit(solution)/shard_map/all_to_all | solution.py:45
  73.9 6.2 %copy-start.3 = (bf16[12,384]{1,0:T(8,128)(2,1)S(1)}, bf16[12,384]{1,0:T(8,128)(2,1)}, u32[]{:S(2)}) copy-start(bf16[12,384]{1,0:T(8,128)(2,1)} %param.15) | copy-start | bytes 27652
  76.6 44.2 %copy-start.1 = (bf16[2,2,64,384]{3,2,1,0:T(8,128)(2,1)S(1)}, bf16[2,2,64,384]{3,2,1,0:T(8,128)(2,1)}, u32[]{:S(2)}) copy-start(bf16[2,2,64,384]{3,2,1,0:T(8,128)(2,1)} %param.13) | copy-start | bytes 589828
  76.6 42.9 %all-to-all-start.2 = ((bf16[8,2,6144]{2,1,0:T(2,128)(2,1)}), bf16[8,2,6144]{2,1,0:T(2,128)(2,1)S(1)}, u32[]{:S(2)}, u32[]{:S(2)}) async-start(bf16[8,2,6144]{2,1,0:T(2,128)(2,1)} %reshape.111), calls=%async_computation.2 | async-start | bytes 393216 | tf_op jit(solution)/shard_map/all_to_all | solution.py:52
where the time goes:
time: 122 us
  blocking collectives  82.9 us (68%)
  local copies, waits for them, and re-layouts  12.4 us (10%)
  starting transfers between devices  12.1 us (10%)
  waiting for transfers between devices  7.98 us (7%)
  matrix products  3.14 us (3%)
  other arithmetic  3.08 us (3%)
    all_gather x1, blocking collectives, body(): lax.all_gather(x_operator, ('mem', 'tile'), axis=0, tiled=True)  43.6 us
    all_gather x1, blocking collectives, body(): lax.all_gather(y_operator, ('mem', 'tile'), axis=0, tiled=True)  39.3 us
    all_to_all x1, waiting for transfers between devices, body(): lax.all_to_all(packed, 'tile', split_axis=0, concat_axis=0, tiled=True)  7.98 us
    all_to_all x1, starting transfers between devices, body(): lax.all_to_all(packed, 'tile', split_axis=0, concat_axis=0, tiled=True)  5.18 us
    all_to_all x1, starting transfers between devices, body(): lax.all_to_all(after_first, 'tile', split_axis=2, concat_axis=3, tiled=True)  3.52 us
    all_to_all x1, starting transfers between devices, body(): lax.all_to_all(difference, 'tile', split_axis=3, concat_axis=2, tiled=True)  3.39 us
    unnamed x19, local copies, waits for them, and re-layouts  3.32 us
  transfers between devices with their start and end apart: 3, of which 1 were waited for; matrix products, arithmetic and copies ran while one was open for 0% of the time, Pallas kernels for 0%

commit v1 on v0

--- a/solution.py
+++ b/solution.py
@@ -3,6 +3,20 @@
 import jax.numpy as jnp
 from jax import lax
 from jax.sharding import PartitionSpec as P
+from jax.lax import axis_index, axis_size, ppermute
+
+
+def perform_wall(q_in):
+    answer = axis_size(("mem", "tile"))
+    kept_arr = axis_index(("mem", "tile"))
+    prior, y, latest = (answer, kept_arr, q_in.shape[0])
+    new, wide_out = (q_in, 1)
+    while wide_out < prior:
+        big = ppermute(new, ("mem", "tile"), [(q, (q - wide_out) % prior) for q in range(prior)])
+        new = jnp.concatenate([new, big], 0)
+        wide_out = 2 * wide_out
+    moved = jnp.roll(new, y * latest, 0)
+    return moved
 
 
 def body(
@@ -51,10 +65,7 @@
     ).astype(jnp.bfloat16)
     tile_back = lax.all_to_all(after_first, "tile", split_axis=2, concat_axis=3, tiled=True)
     after_second = jnp.einsum(
-        "by,mlxy->mlxb",
-        lax.all_gather(y_operator, ("mem", "tile"), axis=0, tiled=True),
-        tile_back,
-        preferred_element_type=jnp.float32,
+        "by,mlxy->mlxb", perform_wall(y_operator), tile_back, preferred_element_type=jnp.float32
     )
     return (regional.astype(jnp.float32) + after_second).astype(jnp.bfloat16)
 

time: 122 us -> 99.4 us (0.81)
  blocking collectives: 82.9 us -> 40.4 us
  starting transfers between devices: 12.1 us -> 26.2 us
  waiting for transfers between devices: 7.98 us -> 12.7 us
    all_gather x1 -> x0, blocking collectives: 39.3 us -> none  [body(): lax.all_gather(y_operator, ('mem', 'tile'), axis=0, tiled=True)]
    ppermute x0 -> x5, waiting for transfers between devices: none -> 12.7 us  [perform_wall(): ppermute(new, ('mem', 'tile'), [(q, (q - wide_out) % prior) for q in rang...]
    ppermute x0 -> x5, starting transfers between devices: none -> 11.3 us  [perform_wall(): ppermute(new, ('mem', 'tile'), [(q, (q - wide_out) % prior) for q in rang...]
    all_to_all x1, waiting for transfers between devices: 7.98 us -> 0.01 us  [body(): lax.all_to_all(packed, 'tile', split_axis=0, concat_axis=0, tiled=True)]
    all_gather x1, blocking collectives: 43.6 us -> 40.4 us  [body(): lax.all_gather(x_operator, ('mem', 'tile'), axis=0, tiled=True)]
    all_to_all x1, starting transfers between devices: 3.39 us -> 6.34 us  [body(): lax.all_to_all(difference, 'tile', split_axis=3, concat_axis=2, tiled=True)]
    unnamed x19 -> x18, local copies, waits for them, and re-layouts: 3.32 us -> 3.25 us
  transfers between devices with their start and end apart: 3 -> 8, of which waited for: 1 -> 3; matrix products, arithmetic and copies ran while one was open for 0% -> 13% of each run, Pallas kernels for 0% -> 0%
where the time goes in v1:
time: 99.4 us; the launch traced here: 98.9 us
  blocking collectives  40.4 us (41%)
  starting transfers between devices  26.2 us (26%)
  local copies, waits for them, and re-layouts  13.1 us (13%)
  waiting for transfers between devices  12.7 us (13%)
  matrix products  3.18 us (3%)
  other arithmetic  3.13 us (3%)
    all_gather x1, blocking collectives, body(): lax.all_gather(x_operator, ('mem', 'tile'), axis=0, tiled=True)  40.4 us
    ppermute x5, waiting for transfers between devices, perform_wall(): ppermute(new, ('mem', 'tile'), [(q, (q - wide_out) % prior) for q in rang...  12.7 us
    ppermute x5, starting transfers between devices, perform_wall(): ppermute(new, ('mem', 'tile'), [(q, (q - wide_out) % prior) for q in rang...  11.3 us
    all_to_all x1, starting transfers between devices, body(): lax.all_to_all(difference, 'tile', split_axis=3, concat_axis=2, tiled=True)  6.34 us
    all_to_all x1, starting transfers between devices, body(): lax.all_to_all(packed, 'tile', split_axis=0, concat_axis=0, tiled=True)  5.18 us
    all_to_all x1, starting transfers between devices, body(): lax.all_to_all(after_first, 'tile', split_axis=2, concat_axis=3, tiled=True)  3.39 us
    unnamed x18, local copies, waits for them, and re-layouts  3.25 us
    transpose x1, local copies, waits for them, and re-layouts, body(): remapped.transpose(2, 3, 0, 4, 1, 5)  2.25 us
  transfers between devices with their start and end apart: 8, of which 3 were waited for; matrix products, arithmetic and copies ran while one was open for 13% of the time, Pallas kernels for 0%

profile of v1, /device:TPU:0, one launch (start us, length us, event | category | flops | bytes accessed | tf_op | source)
XLA Modules:
  0.0 98.9 jit_solution(18323613092247643148)
XLA Ops:
  0.0 0.0 copy-start
  0.0 0.0 copy-start.2
  0.0 0.0 copy-start.6
  0.0 0.0 copy-start.5
  0.0 0.0 copy-start.4
  0.0 0.8 reshape_squeeze.6
  0.8 0.7 compare_and_fusion
  1.5 0.0 copy-done
  1.5 1.4 %gather_fusion = bf16[192,2,2,256]{3,2,1,0:T(2,128)(2,1)S(1)} fusion(bf16[128,2,2,256]{3,2,1,0:T(2,128)(2,1)S(1)} %copy-done, s32[1024]{0:T(1024)S(1)} %pad_clamp_fusion), kind=kCustom, calls=%fused_computation | custom fusion | bytes 787200 | tf_op jit(solution)/shard_map/jit(_take)/gather | solution.py:31
  3.0 1.2 %broadcast_select_fusion = bf16[8,24,2,2,256]{4,3,2,1,0:T(2,128)(2,1)} fusion(bf16[8,24,2,2,256]{4,3,2,1,0:T(2,128)(2,1)S(1)} %bitcast.58, pred[8,24]{1,0:T(8,128)(4,1)S(1)} %compare_and_fusion), kind=kLoop, calls=%fused_computation.6 | loop fusion | flops 196608 | bytes 786624 | tf_op jit(solution)/shard_map/jit(_take)/select_n | solution.py:31
  4.2 5.2 %all-to-all-start = ((bf16[8,24,2,2,256]{4,3,2,1,0:T(2,128)(2,1)}), bf16[8,24,2,2,256]{4,3,2,1,0:T(2,128)(2,1)S(1)}, u32[]{:S(2)}, u32[]{:S(2)}) async-start(bf16[8,24,2,2,256]{4,3,2,1,0:T(2,128)(2,1)} %broadcast_select_fusion), calls=%async_computation | async-start | bytes 786432 | tf_op jit(solution)/shard_map/all_to_all | solution.py:34
  9.4 0.0 copy-done.2
  9.4 5.7 %collective-permute-start = (bf16[12,384]{1,0:T(8,128)(2,1)S(1)}, bf16[12,384]{1,0:T(8,128)(2,1)S(1)}, u32[]{:S(2)}, u32[]{:S(2)}) collective-permute-start(bf16[12,384]{1,0:T(8,128)(2,1)S(1)} %copy-done.2), channel_id=1, source_target_pairs={{0,31},{1,0},{2,1},{3,2},{4,3},{5,4},{6,5},{7,6},{8,7},{9,8},{10,9... | collective-permute-start | bytes 27656 | tf_op jit(solution)/shard_map/ppermute | solution.py:15
  15.1 0.0 copy-done.6
  15.1 0.1 iota_compare_fusion
  15.2 0.1 lt.54
  15.3 0.0 copy-done.5
  15.3 0.1 squeeze.3
  15.4 1.1 %collective-permute-done = bf16[12,384]{1,0:T(8,128)(2,1)S(1)} collective-permute-done((bf16[12,384]{1,0:T(8,128)(2,1)S(1)}, bf16[12,384]{1,0:T(8,128)(2,1)S(1)}, u32[]{:S(2)}, u32[]{:S(2)}) %collective-permute-start) | collective-permute-done | bytes 9248 | tf_op jit(solution)/shard_map/ppermute | solution.py:15
  16.5 4.0 %collective-permute-start.1 = (bf16[24,384]{1,0:T(8,128)(2,1)S(1)}, bf16[24,384]{1,0:T(8,128)(2,1)S(1)}, u32[]{:S(2)}, u32[]{:S(2)}) collective-permute-start(bf16[24,384]{1,0:T(8,128)(2,1)S(1)} %pad_maximum_fusion.2), channel_id=1, source_target_pairs={{0,30},{1,31},{2,0},{3,1},{4,2},{5,3},{6,4},{7,5},{8,6},{9,7},{10,... | collective-permute-start | bytes 55304 | tf_op jit(solution)/shard_map/ppermute | solution.py:15
  20.5 0.0 copy-done.4
  20.5 0.1 eq.18
  20.6 1.4 %collective-permute-done.1 = bf16[24,384]{1,0:T(8,128)(2,1)S(1)} collective-permute-done((bf16[24,384]{1,0:T(8,128)(2,1)S(1)}, bf16[24,384]{1,0:T(8,128)(2,1)S(1)}, u32[]{:S(2)}, u32[]{:S(2)}) %collective-permute-start.1) | collective-permute-done | bytes 18464 | tf_op jit(solution)/shard_map/ppermute | solution.py:15
  22.0 1.5 %collective-permute-start.2 = (bf16[48,384]{1,0:T(8,128)(2,1)S(1)}, bf16[48,384]{1,0:T(8,128)(2,1)S(1)}, u32[]{:S(2)}, u32[]{:S(2)}) collective-permute-start(bf16[48,384]{1,0:T(8,128)(2,1)S(1)} %pad_maximum_fusion.1), channel_id=1, source_target_pairs={{0,28},{1,29},{2,30},{3,31},{4,0},{5,1},{6,2},{7,3},{8,4},{9,5},{1... | collective-permute-start | bytes 110600 | tf_op jit(solution)/shard_map/ppermute | solution.py:15
  23.4 0.0 all-to-all-done
  23.4 0.3 reshape.92
  23.7 0.2 copy.16
  23.9 1.9 %convolution_bitcast_fusion = f32[2,2,4,16,24,16]{4,5,3,1,0,2:T(8,128)} fusion(bf16[2,2,16,16,192,1]{4,3,2,1,0,5:T(8,128)(2,1)S(1)} %bitcast.54, bf16[192]{0:T(256)(128)(2,1)S(1)} %broadcast_select_fusion.1, s32[4,24]{1,0:T(4,128)S(1)} %multiply_add_fusion, s32[192]{0:T(256)S(1)} %eq.18), kind=kOutput, calls=%fused_computation.1 | convolution fusion | flops 37785600 | bytes 787968 | tf_op jit(solution)/shard_map/dot_general | solution.py:42
  25.8 2.2 %copy.17 = f32[2,2,4,16,24,16]{5,4,3,2,1,0:T(8,128)S(1)} copy(f32[2,2,4,16,24,16]{4,5,3,1,0,2:T(8,128)} %convolution_bitcast_fusion) | data formatting | bytes 786432 | tf_op jit(solution)/shard_map/transpose | solution.py:55
  28.0 0.0 copy-start.3
  28.0 1.6 %reshape.93 = f32[2,2,64,384]{3,2,1,0:T(8,128)} reshape(f32[2,2,4,16,24,16]{5,4,3,2,1,0:T(8,128)S(1)} %copy.17) | data formatting | bytes 786432 | tf_op jit(solution)/shard_map/reshape | solution.py:55
  29.7 1.1 %fusion.3 = bf16[2,2,64,384]{3,2,1,0:T(8,128)(2,1)S(1)} fusion(f32[2,2,64,384]{3,2,1,0:T(8,128)} %reshape.93, bf16[2,2,64,384]{3,2,1,0:T(8,128)(2,1)} %param.13), kind=kLoop, calls=%fused_computation.10 | loop fusion | flops 294912 | bytes 786432 | tf_op jit(solution)/shard_map/convert_element_type | solution.py:58
  30.8 0.6 copy.18
  31.4 1.0 reshape.106
  32.4 6.3 %all-to-all-start.1 = ((bf16[8,2,6144]{2,1,0:T(2,128)(2,1)}), bf16[8,2,6144]{2,1,0:T(2,128)(2,1)S(1)}, u32[]{:S(2)}, u32[]{:S(2)}) async-start(bf16[8,2,6144]{2,1,0:T(2,128)(2,1)} %reshape.106), calls=%async_computation.1 | async-start | bytes 393216 | tf_op jit(solution)/shard_map/all_to_all | solution.py:59
  38.7 0.0 copy-done.3
  38.7 40.4 %all_gather.3 = bf16[512,512]{1,0:T(8,128)(2,1)S(1)} all-gather(bf16[16,512]{1,0:T(8,128)(2,1)S(1)} %copy-done.3), channel_id=1, replica_groups=mesh['mem'=4,'tile'=8] {'mem','tile'}, dimensions={0}, use_global_device_ids=true | all-gather | bytes 540672 | tf_op jit(solution)/shard_map/all_gather | solution.py:62
  79.1 0.0 collective-permute-done.2
  79.1 0.1 collective-permute-start.3
  79.2 0.0 all-to-all-done.1
  79.2 0.3 reshape.107
  79.5 0.3 copy.31
  79.8 0.3 all_to_all.33
  80.0 0.3 fusion.1
  80.4 0.4 copy.21
  80.8 1.4 %reshape.108 = bf16[8,2,6144]{2,1,0:T(2,128)(2,1)} reshape(bf16[512,2,2,48]{3,2,1,0:T(2,128)(2,1)S(1)} %bitcast.55) | data formatting | bytes 393216
  82.2 3.4 %all-to-all-start.2 = ((bf16[8,2,6144]{2,1,0:T(2,128)(2,1)}), bf16[8,2,6144]{2,1,0:T(2,128)(2,1)S(1)}, u32[]{:S(2)}, u32[]{:S(2)}) async-start(bf16[8,2,6144]{2,1,0:T(2,128)(2,1)} %reshape.108), calls=%async_computation.2 | async-start | bytes 393216 | tf_op jit(solution)/shard_map/all_to_all | solution.py:66
  85.6 0.0 copy-start.1
  85.6 0.0 collective-permute-done.3
  85.6 0.2 concatenate.25
  85.8 0.1 collective-permute-start.4
  85.9 10.2 %collective-permute-done.4 = bf16[192,384]{1,0:T(8,128)(2,1)S(1)} collective-permute-done((bf16[192,384]{1,0:T(8,128)(2,1)S(1)}, bf16[192,384]{1,0:T(8,128)(2,1)S(1)}, u32[]{:S(2)}, u32[]{:S(2)}) %collective-permute-start.4) | collective-permute-done | bytes 147488 | tf_op jit(solution)/shard_map/ppermute | solution.py:15
  96.1 0.6 concatenate.26
  96.7 0.0 all-to-all-done.2
  96.7 0.5 reshape.109
  97.2 0.3 copy.30
  97.6 0.4 all_to_all.37
  97.9 0.0 copy-done.1
  97.9 1.0 fusion
  (7 shorter events, 0.1 us)
Async XLA Ops:
  0.0 1.5 %copy-start = (bf16[128,2,2,256]{3,2,1,0:T(2,128)(2,1)S(1)}, bf16[128,2,2,256]{3,2,1,0:T(2,128)(2,1)}, u32[]{:S(2)}) copy-start(bf16[128,2,2,256]{3,2,1,0:T(2,128)(2,1)} %param.8) | copy-start | bytes 786436
  0.0 9.4 %copy-start.2 = (bf16[12,384]{1,0:T(8,128)(2,1)S(1)}, bf16[12,384]{1,0:T(8,128)(2,1)}, u32[]{:S(2)}) copy-start(bf16[12,384]{1,0:T(8,128)(2,1)} %param.15) | copy-start | bytes 27652
  0.0 15.1 %copy-start.6 = (s32[1,8]{1,0:T(1,128)S(1)}, s32[1,8]{1,0:T(1,128)}, u32[]{:S(2)}) copy-start(s32[1,8]{1,0:T(1,128)} %param.12) | copy-start | bytes 100
  0.0 15.3 %copy-start.5 = (f32[1,8,24]{2,1,0:T(8,128)S(1)}, f32[1,8,24]{2,1,0:T(8,128)}, u32[]{:S(2)}) copy-start(f32[1,8,24]{2,1,0:T(8,128)} %param.11) | copy-start | bytes 2308
  0.0 20.5 %copy-start.4 = (s32[1,8,24]{2,1,0:T(8,128)S(1)}, s32[1,8,24]{2,1,0:T(8,128)}, u32[]{:S(2)}) copy-start(s32[1,8,24]{2,1,0:T(8,128)} %param.10) | copy-start | bytes 2308
  4.2 19.2 %all-to-all-start = ((bf16[8,24,2,2,256]{4,3,2,1,0:T(2,128)(2,1)}), bf16[8,24,2,2,256]{4,3,2,1,0:T(2,128)(2,1)S(1)}, u32[]{:S(2)}, u32[]{:S(2)}) async-start(bf16[8,24,2,2,256]{4,3,2,1,0:T(2,128)(2,1)} %broadcast_select_fusion), calls=%async_computation | async-start | bytes 786432 | tf_op jit(solution)/shard_map/all_to_all | solution.py:34
  9.4 7.1 %collective-permute-start = (bf16[12,384]{1,0:T(8,128)(2,1)S(1)}, bf16[12,384]{1,0:T(8,128)(2,1)S(1)}, u32[]{:S(2)}, u32[]{:S(2)}) collective-permute-start(bf16[12,384]{1,0:T(8,128)(2,1)S(1)} %copy-done.2), channel_id=1, source_target_pairs={{0,31},{1,0},{2,1},{3,2},{4,3},{5,4},{6,5},{7,6},{8,7},{9,8},{10,9... | collective-permute-start | bytes 27656 | tf_op jit(solution)/shard_map/ppermute | solution.py:15
  16.5 5.4 %collective-permute-start.1 = (bf16[24,384]{1,0:T(8,128)(2,1)S(1)}, bf16[24,384]{1,0:T(8,128)(2,1)S(1)}, u32[]{:S(2)}, u32[]{:S(2)}) collective-permute-start(bf16[24,384]{1,0:T(8,128)(2,1)S(1)} %pad_maximum_fusion.2), channel_id=1, source_target_pairs={{0,30},{1,31},{2,0},{3,1},{4,2},{5,3},{6,4},{7,5},{8,6},{9,7},{10,... | collective-permute-start | bytes 55304 | tf_op jit(solution)/shard_map/ppermute | solution.py:15
  22.0 57.1 %collective-permute-start.2 = (bf16[48,384]{1,0:T(8,128)(2,1)S(1)}, bf16[48,384]{1,0:T(8,128)(2,1)S(1)}, u32[]{:S(2)}, u32[]{:S(2)}) collective-permute-start(bf16[48,384]{1,0:T(8,128)(2,1)S(1)} %pad_maximum_fusion.1), channel_id=1, source_target_pairs={{0,28},{1,29},{2,30},{3,31},{4,0},{5,1},{6,2},{7,3},{8,4},{9,5},{1... | collective-permute-start | bytes 110600 | tf_op jit(solution)/shard_map/ppermute | solution.py:15
  28.0 10.7 %copy-start.3 = (bf16[16,512]{1,0:T(8,128)(2,1)S(1)}, bf16[16,512]{1,0:T(8,128)(2,1)}, u32[]{:S(2)}) copy-start(bf16[16,512]{1,0:T(8,128)(2,1)} %param.14) | copy-start | bytes 49156
  32.4 46.8 %all-to-all-start.1 = ((bf16[8,2,6144]{2,1,0:T(2,128)(2,1)}), bf16[8,2,6144]{2,1,0:T(2,128)(2,1)S(1)}, u32[]{:S(2)}, u32[]{:S(2)}) async-start(bf16[8,2,6144]{2,1,0:T(2,128)(2,1)} %reshape.106), calls=%async_computation.1 | async-start | bytes 393216 | tf_op jit(solution)/shard_map/all_to_all | solution.py:59
  79.1 6.5 %collective-permute-start.3 = (bf16[96,384]{1,0:T(8,128)(2,1)S(1)}, bf16[96,384]{1,0:T(8,128)(2,1)S(1)}, u32[]{:S(2)}, u32[]{:S(2)}) collective-permute-start(bf16[96,384]{1,0:T(8,128)(2,1)S(1)} %pad_maximum_fusion), channel_id=1, source_target_pairs={{0,24},{1,25},{2,26},{3,27},{4,28},{5,29},{6,30},{7,31},{8,0},{9,1... | collective-permute-start | bytes 221192 | tf_op jit(solution)/shard_map/ppermute | solution.py:15
  82.2 14.5 %all-to-all-start.2 = ((bf16[8,2,6144]{2,1,0:T(2,128)(2,1)}), bf16[8,2,6144]{2,1,0:T(2,128)(2,1)S(1)}, u32[]{:S(2)}, u32[]{:S(2)}) async-start(bf16[8,2,6144]{2,1,0:T(2,128)(2,1)} %reshape.108), calls=%async_computation.2 | async-start | bytes 393216 | tf_op jit(solution)/shard_map/all_to_all | solution.py:66
  85.6 12.3 %copy-start.1 = (bf16[2,2,64,384]{3,2,1,0:T(8,128)(2,1)S(1)}, bf16[2,2,64,384]{3,2,1,0:T(8,128)(2,1)}, u32[]{:S(2)}) copy-start(bf16[2,2,64,384]{3,2,1,0:T(8,128)(2,1)} %param.13) | copy-start | bytes 589828
  85.8 10.3 %collective-permute-start.4 = (bf16[192,384]{1,0:T(8,128)(2,1)S(1)}, bf16[192,384]{1,0:T(8,128)(2,1)S(1)}, u32[]{:S(2)}, u32[]{:S(2)}) collective-permute-start(bf16[192,384]{1,0:T(8,128)(2,1)S(1)} %concatenate.25), channel_id=1, source_target_pairs={{0,16},{1,17},{2,18},{3,19},{4,20},{5,21},{6,22},{7,23},{8,24},{9,... | collective-permute-start | bytes 442376 | tf_op jit(solution)/shard_map/ppermute | solution.py:15
